TPU v7x, 128 devices: a whole 4x4x4 slice. The times are simulated.
128 devices in a mesh: clu: 8 (over y, x_hi), mem: 16 (over x_lo, z, core).
Axes of the slice: x: 4 (x_hi: 2, x_lo: 2; x = x_hi * 2 + x_lo), y: 4, z: 4, core: 2. Of those that a mesh axis runs over, the one named last changes fastest.
Arguments:
- embeddings: bfloat16 [131072, 768], P(('clu', 'mem'))
- block_order: int32 [8, 128], P('clu'), may hold values from 0 to 7, as said below
Outputs:
- weight: float32 [131072], P(('clu', 'mem'))
Inputs may be any that keep to these rules, and one draw needn't show every extreme that they name: `block_order`: each aligned run of 8 entries is a permutation of 0 to 7.
All inputs are finite; a program needn't handle non-finite values.
Results may differ from a plain program's by a relative error of at most 0.0029.
Values may be sent and summed in bfloat16 or wider, within the bound.
No kernel may reach another device: no remote copies, remote signals or barrier semaphores. Data moves between devices by JAX's collectives and lax.ppermute only.
A program may use at most 64 MiB of HBM per device.

v0:
```python
import jax
import jax.numpy as jnp
from jax import lax
from jax.sharding import PartitionSpec as P

BLK = 128


def squared(values):
    return jnp.sum(jnp.square(values.astype(jnp.float32)), axis=1)


def class_table(count):
    spots = jnp.arange(count, dtype=jnp.int32)
    levels = count.bit_length() - 1
    classes = jnp.zeros((count,), jnp.int32)
    for level in range(1, levels + 1):
        classes = classes + (spots >= count - (count >> level)).astype(jnp.int32)
    return classes


def shards(embeddings, block_order):
    row_count = embeddings.shape[0]
    member_count = lax.axis_size("mem")
    position = lax.axis_index("mem")
    per_device = row_count // BLK
    orders = block_order[0].reshape(member_count, per_device)
    classes = class_table(per_device)
    locals_range = jnp.arange(per_device, dtype=jnp.int32)
    matches = (orders[:, :, None] == locals_range[None, None, :]).astype(jnp.int32)
    group_ids = jnp.sum(matches * classes[None, :, None], axis=1).reshape(-1)
    own_ids = jnp.repeat(
        lax.dynamic_slice_in_dim(group_ids, position * per_device, per_device), BLK
    )
    own_norms = squared(embeddings)

    def kernel_tile(other, other_row):
        other_ids = jnp.repeat(
            lax.dynamic_slice_in_dim(group_ids, other_row // BLK, per_device), BLK
        )
        products = lax.dot_general(
            embeddings, other, (((1,), (1,)), ((), ())), preferred_element_type=jnp.float32
        )
        distance = own_norms[:, None] + squared(other)[None, :] - 2.0 * products
        return jnp.where(
            own_ids[:, None] == other_ids[None, :], jnp.exp(-0.5 * distance), jnp.float32(0.0)
        )

    pieces = lax.all_gather(embeddings, "mem", axis=0, tiled=True)
    shard_count = pieces.shape[0] // row_count

    def add_shard(shard_index, running):
        shard = lax.dynamic_slice_in_dim(pieces, shard_index * row_count, row_count, 0)
        return running + jnp.sum(kernel_tile(shard, shard_index * row_count), axis=1)

    density = lax.fori_loop(0, shard_count, add_shard, jnp.zeros((row_count,), jnp.float32))
    inverse = 1.0 / density
    total = lax.psum(jnp.sum(inverse), ("clu", "mem"))
    everything = jnp.float32(row_count * lax.axis_size("clu") * member_count)
    return inverse * (everything / total)


def solution(mesh):
    placed = (P(("clu", "mem"), None), P("clu", None))
    return jax.shard_map(
        shards, mesh=mesh, in_specs=placed, out_specs=P(("clu", "mem")), check_vma=False
    )
```

profile of v0, /device:TPU:0, one launch (start us, length us, event | category | flops | bytes accessed | tf_op | source)
XLA Modules:
  0.0 317.5 jit_solution(4564834575128845005)
XLA Ops:
  9.6 1.8 multiply_reduce_fusion.1
  11.4 131.3 %all-gather.2.cloned.1.call-done = bf16[16384,768]{1,0:T(8,128)(2,1)} async-done(((bf16[1024,768]{1,0:T(8,128)(2,1)}), bf16[16384,768]{1,0:T(8,128)(2,1)}) %all-gather.2.cloned.1.call-update) | async-done | bytes 25165840 | tf_op jit(solution)/shard_map/all_gather | solution.py:49
  142.7 99.9 %while.16 = (s32[]{:T(128)}, f32[1024]{0:T(1024)S(1)}, s32[128]{0:T(128)S(1)}, f32[1024]{0:T(1024)S(1)}, bf16[16384,768]{1,0:T(8,128)(2,1)}, /*index=5*/bf16[102...) while((s32[]{:T(128)}, f32[1024]{0:T(1024)S(1)}, ...), condition=%wide.region_5.6_spmd.clone, body=%wide.region_2.5_spmd.clone.sunk | while | flops 1620312064 | bytes 4764160 | solution.py:56
  144.6 4.2 %fusion.17 = f32[1024]{0:T(1024)S(1)} fusion(bf16[1024,768]{1,0:T(8,128)(2,1)} %get-tuple-element.308, f32[1024]{0:T(1024)S(1)} %multiply_reduce_fusion.3, f32[1024]{0:T(1024)S(1)} %get-tuple-element.306, s32[1024]{0:T(1024)S(1)} %get-tuple-element.271, s32[1024]{0:T(1024)S(1)} %get-tuple-element.272, bf16[16384,768]{1,0:T(8,128)(2,1)} %get-tuple-element.307, ...), kind=kOutput, calls=%fused_computation.5.clone.1 | convolution fusion | flops 1617951744 | bytes 3166212 | tf_op jit(solution)/shard_map/while/body/eval_jaxpr/dot_general | solution.py:41
  149.1 1.8 multiply_reduce_fusion.3
  150.8 4.2 %fusion.17 = f32[1024]{0:T(1024)S(1)} fusion(bf16[1024,768]{1,0:T(8,128)(2,1)} %get-tuple-element.308, f32[1024]{0:T(1024)S(1)} %multiply_reduce_fusion.3, f32[1024]{0:T(1024)S(1)} %get-tuple-element.306, s32[1024]{0:T(1024)S(1)} %get-tuple-element.271, s32[1024]{0:T(1024)S(1)} %get-tuple-element.272, bf16[16384,768]{1,0:T(8,128)(2,1)} %get-tuple-element.307, ...), kind=kOutput, calls=%fused_computation.5.clone.1 | convolution fusion | flops 1617951744 | bytes 3166212 | tf_op jit(solution)/shard_map/while/body/eval_jaxpr/dot_general | solution.py:41
  155.3 1.8 multiply_reduce_fusion.3
  157.1 4.2 %fusion.17 = f32[1024]{0:T(1024)S(1)} fusion(bf16[1024,768]{1,0:T(8,128)(2,1)} %get-tuple-element.308, f32[1024]{0:T(1024)S(1)} %multiply_reduce_fusion.3, f32[1024]{0:T(1024)S(1)} %get-tuple-element.306, s32[1024]{0:T(1024)S(1)} %get-tuple-element.271, s32[1024]{0:T(1024)S(1)} %get-tuple-element.272, bf16[16384,768]{1,0:T(8,128)(2,1)} %get-tuple-element.307, ...), kind=kOutput, calls=%fused_computation.5.clone.1 | convolution fusion | flops 1617951744 | bytes 3166212 | tf_op jit(solution)/shard_map/while/body/eval_jaxpr/dot_general | solution.py:41
  163.3 4.2 %fusion.17 = f32[1024]{0:T(1024)S(1)} fusion(bf16[1024,768]{1,0:T(8,128)(2,1)} %get-tuple-element.308, f32[1024]{0:T(1024)S(1)} %multiply_reduce_fusion.3, f32[1024]{0:T(1024)S(1)} %get-tuple-element.306, s32[1024]{0:T(1024)S(1)} %get-tuple-element.271, s32[1024]{0:T(1024)S(1)} %get-tuple-element.272, bf16[16384,768]{1,0:T(8,128)(2,1)} %get-tuple-element.307, ...), kind=kOutput, calls=%fused_computation.5.clone.1 | convolution fusion | flops 1617951744 | bytes 3166212 | tf_op jit(solution)/shard_map/while/body/eval_jaxpr/dot_general | solution.py:41
  169.6 4.2 %fusion.17 = f32[1024]{0:T(1024)S(1)} fusion(bf16[1024,768]{1,0:T(8,128)(2,1)} %get-tuple-element.308, f32[1024]{0:T(1024)S(1)} %multiply_reduce_fusion.3, f32[1024]{0:T(1024)S(1)} %get-tuple-element.306, s32[1024]{0:T(1024)S(1)} %get-tuple-element.271, s32[1024]{0:T(1024)S(1)} %get-tuple-element.272, bf16[16384,768]{1,0:T(8,128)(2,1)} %get-tuple-element.307, ...), kind=kOutput, calls=%fused_computation.5.clone.1 | convolution fusion | flops 1617951744 | bytes 3166212 | tf_op jit(solution)/shard_map/while/body/eval_jaxpr/dot_general | solution.py:41
  175.8 4.2 %fusion.17 = f32[1024]{0:T(1024)S(1)} fusion(bf16[1024,768]{1,0:T(8,128)(2,1)} %get-tuple-element.308, f32[1024]{0:T(1024)S(1)} %multiply_reduce_fusion.3, f32[1024]{0:T(1024)S(1)} %get-tuple-element.306, s32[1024]{0:T(1024)S(1)} %get-tuple-element.271, s32[1024]{0:T(1024)S(1)} %get-tuple-element.272, bf16[16384,768]{1,0:T(8,128)(2,1)} %get-tuple-element.307, ...), kind=kOutput, calls=%fused_computation.5.clone.1 | convolution fusion | flops 1617951744 | bytes 3166212 | tf_op jit(solution)/shard_map/while/body/eval_jaxpr/dot_general | solution.py:41
  180.3 1.8 multiply_reduce_fusion.3
  182.1 4.2 %fusion.17 = f32[1024]{0:T(1024)S(1)} fusion(bf16[1024,768]{1,0:T(8,128)(2,1)} %get-tuple-element.308, f32[1024]{0:T(1024)S(1)} %multiply_reduce_fusion.3, f32[1024]{0:T(1024)S(1)} %get-tuple-element.306, s32[1024]{0:T(1024)S(1)} %get-tuple-element.271, s32[1024]{0:T(1024)S(1)} %get-tuple-element.272, bf16[16384,768]{1,0:T(8,128)(2,1)} %get-tuple-element.307, ...), kind=kOutput, calls=%fused_computation.5.clone.1 | convolution fusion | flops 1617951744 | bytes 3166212 | tf_op jit(solution)/shard_map/while/body/eval_jaxpr/dot_general | solution.py:41
  186.5 1.8 multiply_reduce_fusion.3
  188.3 4.2 %fusion.17 = f32[1024]{0:T(1024)S(1)} fusion(bf16[1024,768]{1,0:T(8,128)(2,1)} %get-tuple-element.308, f32[1024]{0:T(1024)S(1)} %multiply_reduce_fusion.3, f32[1024]{0:T(1024)S(1)} %get-tuple-element.306, s32[1024]{0:T(1024)S(1)} %get-tuple-element.271, s32[1024]{0:T(1024)S(1)} %get-tuple-element.272, bf16[16384,768]{1,0:T(8,128)(2,1)} %get-tuple-element.307, ...), kind=kOutput, calls=%fused_computation.5.clone.1 | convolution fusion | flops 1617951744 | bytes 3166212 | tf_op jit(solution)/shard_map/while/body/eval_jaxpr/dot_general | solution.py:41
  192.8 1.8 multiply_reduce_fusion.3
  194.6 4.2 %fusion.17 = f32[1024]{0:T(1024)S(1)} fusion(bf16[1024,768]{1,0:T(8,128)(2,1)} %get-tuple-element.308, f32[1024]{0:T(1024)S(1)} %multiply_reduce_fusion.3, f32[1024]{0:T(1024)S(1)} %get-tuple-element.306, s32[1024]{0:T(1024)S(1)} %get-tuple-element.271, s32[1024]{0:T(1024)S(1)} %get-tuple-element.272, bf16[16384,768]{1,0:T(8,128)(2,1)} %get-tuple-element.307, ...), kind=kOutput, calls=%fused_computation.5.clone.1 | convolution fusion | flops 1617951744 | bytes 3166212 | tf_op jit(solution)/shard_map/while/body/eval_jaxpr/dot_general | solution.py:41
  199.0 1.8 multiply_reduce_fusion.3
  200.8 4.2 %fusion.17 = f32[1024]{0:T(1024)S(1)} fusion(bf16[1024,768]{1,0:T(8,128)(2,1)} %get-tuple-element.308, f32[1024]{0:T(1024)S(1)} %multiply_reduce_fusion.3, f32[1024]{0:T(1024)S(1)} %get-tuple-element.306, s32[1024]{0:T(1024)S(1)} %get-tuple-element.271, s32[1024]{0:T(1024)S(1)} %get-tuple-element.272, bf16[16384,768]{1,0:T(8,128)(2,1)} %get-tuple-element.307, ...), kind=kOutput, calls=%fused_computation.5.clone.1 | convolution fusion | flops 1617951744 | bytes 3166212 | tf_op jit(solution)/shard_map/while/body/eval_jaxpr/dot_general | solution.py:41
  205.3 1.8 multiply_reduce_fusion.3
  207.1 4.2 %fusion.17 = f32[1024]{0:T(1024)S(1)} fusion(bf16[1024,768]{1,0:T(8,128)(2,1)} %get-tuple-element.308, f32[1024]{0:T(1024)S(1)} %multiply_reduce_fusion.3, f32[1024]{0:T(1024)S(1)} %get-tuple-element.306, s32[1024]{0:T(1024)S(1)} %get-tuple-element.271, s32[1024]{0:T(1024)S(1)} %get-tuple-element.272, bf16[16384,768]{1,0:T(8,128)(2,1)} %get-tuple-element.307, ...), kind=kOutput, calls=%fused_computation.5.clone.1 | convolution fusion | flops 1617951744 | bytes 3166212 | tf_op jit(solution)/shard_map/while/body/eval_jaxpr/dot_general | solution.py:41
  211.5 1.8 multiply_reduce_fusion.3
  213.3 4.2 %fusion.17 = f32[1024]{0:T(1024)S(1)} fusion(bf16[1024,768]{1,0:T(8,128)(2,1)} %get-tuple-element.308, f32[1024]{0:T(1024)S(1)} %multiply_reduce_fusion.3, f32[1024]{0:T(1024)S(1)} %get-tuple-element.306, s32[1024]{0:T(1024)S(1)} %get-tuple-element.271, s32[1024]{0:T(1024)S(1)} %get-tuple-element.272, bf16[16384,768]{1,0:T(8,128)(2,1)} %get-tuple-element.307, ...), kind=kOutput, calls=%fused_computation.5.clone.1 | convolution fusion | flops 1617951744 | bytes 3166212 | tf_op jit(solution)/shard_map/while/body/eval_jaxpr/dot_general | solution.py:41
  217.8 1.8 multiply_reduce_fusion.3
  219.6 4.2 %fusion.17 = f32[1024]{0:T(1024)S(1)} fusion(bf16[1024,768]{1,0:T(8,128)(2,1)} %get-tuple-element.308, f32[1024]{0:T(1024)S(1)} %multiply_reduce_fusion.3, f32[1024]{0:T(1024)S(1)} %get-tuple-element.306, s32[1024]{0:T(1024)S(1)} %get-tuple-element.271, s32[1024]{0:T(1024)S(1)} %get-tuple-element.272, bf16[16384,768]{1,0:T(8,128)(2,1)} %get-tuple-element.307, ...), kind=kOutput, calls=%fused_computation.5.clone.1 | convolution fusion | flops 1617951744 | bytes 3166212 | tf_op jit(solution)/shard_map/while/body/eval_jaxpr/dot_general | solution.py:41
  224.0 1.8 multiply_reduce_fusion.3
  225.8 4.2 %fusion.17 = f32[1024]{0:T(1024)S(1)} fusion(bf16[1024,768]{1,0:T(8,128)(2,1)} %get-tuple-element.308, f32[1024]{0:T(1024)S(1)} %multiply_reduce_fusion.3, f32[1024]{0:T(1024)S(1)} %get-tuple-element.306, s32[1024]{0:T(1024)S(1)} %get-tuple-element.271, s32[1024]{0:T(1024)S(1)} %get-tuple-element.272, bf16[16384,768]{1,0:T(8,128)(2,1)} %get-tuple-element.307, ...), kind=kOutput, calls=%fused_computation.5.clone.1 | convolution fusion | flops 1617951744 | bytes 3166212 | tf_op jit(solution)/shard_map/while/body/eval_jaxpr/dot_general | solution.py:41
  230.3 1.8 multiply_reduce_fusion.3
  232.1 4.2 %fusion.17 = f32[1024]{0:T(1024)S(1)} fusion(bf16[1024,768]{1,0:T(8,128)(2,1)} %get-tuple-element.308, f32[1024]{0:T(1024)S(1)} %multiply_reduce_fusion.3, f32[1024]{0:T(1024)S(1)} %get-tuple-element.306, s32[1024]{0:T(1024)S(1)} %get-tuple-element.271, s32[1024]{0:T(1024)S(1)} %get-tuple-element.272, bf16[16384,768]{1,0:T(8,128)(2,1)} %get-tuple-element.307, ...), kind=kOutput, calls=%fused_computation.5.clone.1 | convolution fusion | flops 1617951744 | bytes 3166212 | tf_op jit(solution)/shard_map/while/body/eval_jaxpr/dot_general | solution.py:41
  236.5 1.8 multiply_reduce_fusion.3
  238.3 4.2 %fusion.17 = f32[1024]{0:T(1024)S(1)} fusion(bf16[1024,768]{1,0:T(8,128)(2,1)} %get-tuple-element.308, f32[1024]{0:T(1024)S(1)} %multiply_reduce_fusion.3, f32[1024]{0:T(1024)S(1)} %get-tuple-element.306, s32[1024]{0:T(1024)S(1)} %get-tuple-element.271, s32[1024]{0:T(1024)S(1)} %get-tuple-element.272, bf16[16384,768]{1,0:T(8,128)(2,1)} %get-tuple-element.307, ...), kind=kOutput, calls=%fused_computation.5.clone.1 | convolution fusion | flops 1617951744 | bytes 3166212 | tf_op jit(solution)/shard_map/while/body/eval_jaxpr/dot_general | solution.py:41
  243.2 66.1 %psum.7 = f32[]{:T(128)} all-reduce(f32[]{:T(128)} %fusion.8), channel_id=1, replica_groups=mesh['clu'=8,'mem'=16] {'clu','mem'}, use_global_device_ids=true, to_apply=%region_7.8 | all-reduce | flops 1 | bytes 8 | tf_op jit(solution)/shard_map/psum | solution.py:58
  (66 shorter events, 13.9 us)
Async XLA Ops:
  6.5 136.1 %all-gather.2.cloned.1.call-start = ((), (), s32[]{:S(2)}) async-start(), calls=%async_computation | async-start | bytes 26738688 | tf_op jit(solution)/shard_map/all_gather | solution.py:49
Sparse Core Ops, SparseCore 0:
  9.0 133.5 all-gather.1
where the time goes:
time: 319 us; the launch traced here: 317 us
  waiting for transfers between devices  132 us (41%)
  matrix products  67.8 us (21%)
  blocking collectives  66.1 us (21%)
  other arithmetic  33 us (10%)
  between operations  14.1 us (4%)
  local copies, waits for them, and re-layouts  3.31 us (1%)
    all_gather x1, waiting for transfers between devices, shards(): pieces = lax.all_gather(embeddings, 'mem', axis=0, tiled=True)  131 us
    dot_general x16, matrix products, kernel_tile(): lax.dot_general(embeddings, other, (((1,), (1,)), ((), ())), preferred_el...  67.8 us
    psum x1, blocking collectives, shards(): total = lax.psum(jnp.sum(inverse), ('clu', 'mem'))  66.1 us
    reduce_sum x17, other arithmetic, squared(): return jnp.sum(jnp.square(values.astype(jnp.float32)), axis=1)  30.3 us
  transfers between devices with their start and end apart: 1, of which 1 were waited for; matrix products, arithmetic and copies ran while one was open for 1% of the time, Pallas kernels for 0%

commit v1 on v0

v1 whole, which is shorter than its diff:
```python
import jax
import jax.numpy as jnp
from jax import lax
from jax.sharding import PartitionSpec as P

BLK = 128


def squared(values):
    return jnp.sum(jnp.square(values.astype(jnp.float32)), axis=1)


def class_table(count):
    spots = jnp.arange(count, dtype=jnp.int32)
    levels = count.bit_length() - 1
    classes = jnp.zeros((count,), jnp.int32)
    for level in range(1, levels + 1):
        classes = classes + (spots >= count - (count >> level)).astype(jnp.int32)
    return classes


def class_spans(count):
    spans = []
    start = 0
    width = count // 2
    while start < count:
        end = min(start + max(width, 1), count)
        spans.append((start, end))
        start = end
        width //= 2
    return spans


def pieces_of(spans, most):
    pieces = []
    for index, (start, end) in enumerate(spans):
        while start < end:
            stop = min(start + most, end)
            pieces.append((index, start, stop))
            start = stop
    return pieces


def tree_total(value, axis, size):
    stride = 1
    while stride < size:
        if stride * 4 <= size:
            def swap(k):
                return lax.ppermute(value, axis, [(i, i ^ k) for i in range(size)])
            one, two, three = swap(stride), swap(2 * stride), swap(3 * stride)
            value = (value + one) + (two + three)
            stride *= 4
        else:
            value = value + lax.ppermute(value, axis, [(i, i ^ stride) for i in range(size)])
            stride *= 2
    return value


def shards(embeddings, block_order):
    row_count, width = embeddings.shape
    member_count = lax.axis_size("mem")
    position = lax.axis_index("mem")
    per_device = row_count // BLK
    order = lax.dynamic_slice_in_dim(block_order[0], position * per_device, per_device)
    blocks = embeddings.reshape(per_device, BLK, width)
    ordered = jnp.take(blocks, order, axis=0)
    spans = class_spans(per_device)
    pieces = pieces_of(spans, max(per_device // 4, 1))

    own = [ordered[start:end].reshape(-1, width) for start, end in spans]
    own_norms = [squared(rows) for rows in own]
    density = [jnp.zeros((rows.shape[0],), jnp.float32) for rows in own]
    for index, start, stop in pieces:
        other = lax.all_gather(ordered[start:stop].reshape(-1, width), "mem", axis=0, tiled=True)
        products = lax.dot_general(
            own[index], other, (((1,), (1,)), ((), ())), preferred_element_type=jnp.float32
        )
        distance = own_norms[index][:, None] + squared(other)[None, :] - 2.0 * products
        density[index] = density[index] + jnp.sum(jnp.exp(-0.5 * distance), axis=1)

    inverse = 1.0 / jnp.concatenate(density).reshape(per_device, BLK)
    total = tree_total(jnp.sum(inverse), "mem", member_count)
    total = tree_total(total, "clu", lax.axis_size("clu"))
    everything = jnp.float32(row_count * lax.axis_size("clu") * member_count)
    weight = inverse * (everything / total)
    spots = jnp.arange(per_device, dtype=jnp.int32)
    back = jnp.sum(
        jnp.where(order[None, :] == spots[:, None], spots[None, :], 0), axis=1
    )
    return jnp.take(weight, back, axis=0).reshape(-1)


def solution(mesh):
    placed = (P(("clu", "mem"), None), P("clu", None))
    return jax.shard_map(
        shards, mesh=mesh, in_specs=placed, out_specs=P(("clu", "mem")), check_vma=False
    )
```

time: 319 us -> 276 us (0.87)
  blocking collectives: 66.1 us -> 0 us
  waiting for transfers between devices: 132 us -> 188 us
  matrix products: 67.8 us -> 14.9 us
  starting transfers between devices: 0.01 us -> 24 us
  other arithmetic: 33 us -> 23 us
  between operations: 14.1 us -> 20.4 us
    psum x1 -> x0, blocking collectives: 66.1 us -> none  [shards(): total = lax.psum(jnp.sum(inverse), ('clu', 'mem'))]
    dot_general x16 -> x5, matrix products: 67.8 us -> 14.9 us  [shards(): lax.dot_general(own[index], other, (((1,), (1,)), ((), ())), preferred_el...]
    all_gather x1 -> x5, waiting for transfers between devices: 131 us -> 177 us  [shards(): lax.all_gather(ordered[start:stop].reshape(-1, width), 'mem', axis=0, til...]
    ppermute x0 -> x10, starting transfers between devices: none -> 23.9 us  [the longest x9 19.8 us: swap(): return lax.ppermute(value, axis, [(i, i ^ k) for i in range(size)])]
    reduce_sum x17 -> x8, other arithmetic: 30.3 us -> 18.4 us  [squared(): return jnp.sum(jnp.square(values.astype(jnp.float32)), axis=1)]
    ppermute x0 -> x10, waiting for transfers between devices: none -> 8.43 us  [the longest x9 7.43 us: swap(): return lax.ppermute(value, axis, [(i, i ^ k) for i in range(size)])]
  transfers between devices with their start and end apart: 1 -> 15, of which waited for: 1 -> 10; matrix products, arithmetic and copies ran while one was open for 1% -> 11% of each run, Pallas kernels for 0% -> 0%
where the time goes in v1:
time: 276 us
  waiting for transfers between devices  188 us (68%)
  starting transfers between devices  24 us (9%)
  other arithmetic  23 us (8%)
  between operations  20.4 us (7%)
  matrix products  14.9 us (5%)
  local copies, waits for them, and re-layouts  5.91 us (2%)
    all_gather x5, waiting for transfers between devices, shards(): lax.all_gather(ordered[start:stop].reshape(-1, width), 'mem', axis=0, til...  177 us
    ppermute x9, starting transfers between devices, swap(): return lax.ppermute(value, axis, [(i, i ^ k) for i in range(size)])  19.8 us
    reduce_sum x8, other arithmetic, squared(): return jnp.sum(jnp.square(values.astype(jnp.float32)), axis=1)  18.4 us
    dot_general x5, matrix products, shards(): lax.dot_general(own[index], other, (((1,), (1,)), ((), ())), preferred_el...  14.9 us
    ppermute x9, waiting for transfers between devices, swap(): return lax.ppermute(value, axis, [(i, i ^ k) for i in range(size)])  7.43 us
  transfers between devices with their start and end apart: 15, of which 10 were waited for; matrix products, arithmetic and copies ran while one was open for 11% of the time, Pallas kernels for 0%

profile of v1, /device:TPU:0, one launch (start us, length us, event | category | flops | bytes accessed | tf_op | source)
XLA Modules:
  0.0 276.0 jit_solution(18131353465139840405)
XLA Ops:
  6.5 0.8 fusion.40
  8.1 1.8 gather_fusion
  9.9 1.6 broadcast_select_fusion
  13.2 1.0 fusion.47
  15.4 1.0 slice.31
  17.1 33.5 %all-gather.16.cloned.1.call-done = bf16[1,2048,768]{2,1,0:T(8,128)(2,1)} async-done(((bf16[1,128,768]{2,1,0:T(8,128)(2,1)}), bf16[1,2048,768]{2,1,0:T(8,128)(2,1)}) %all-gather.16.cloned.1.call-update) | async-done | bytes 3145744 | tf_op jit(solution)/shard_map/all_gather | solution.py:74
  50.6 2.6 multiply_reduce_fusion.3
  53.2 34.6 %all-gather.14.cloned.1.call-done = bf16[1,2048,768]{2,1,0:T(8,128)(2,1)} async-done(((bf16[1,128,768]{2,1,0:T(8,128)(2,1)}), bf16[1,2048,768]{2,1,0:T(8,128)(2,1)}) %all-gather.14.cloned.1.call-update) | async-done | bytes 3145744 | tf_op jit(solution)/shard_map/all_gather | solution.py:74
  87.8 2.7 multiply_reduce_fusion.4
  90.5 3.1 %fusion.32 = f32[128]{0:T(128)S(1)} fusion(bf16[1,2048,768]{2,1,0:T(8,128)(2,1)} %all-gather.16.cloned.1.call-done, f32[2048]{0:T(1024)S(1)} %multiply_reduce_fusion.3, f32[128]{0:T(128)S(1)} %get-tuple-element.6, bf16[8,128,768]{2,1,0:T(8,128)(2,1)S(1)} %broadcast_select_fusion), kind=kOutput, calls=%fused_computation.28 | convolution fusion | flops 403963776 | bytes 3351552 | tf_op jit(solution)/shard_map/dot_general | solution.py:75
  93.7 1.3 fusion.35
  94.9 36.9 %all-gather.8.cloned.1.call-done = bf16[4096,768]{1,0:T(8,128)(2,1)} async-done(((bf16[256,768]{1,0:T(8,128)(2,1)}), bf16[4096,768]{1,0:T(8,128)(2,1)}) %all-gather.8.cloned.1.call-update) | async-done | bytes 6291472 | tf_op jit(solution)/shard_map/all_gather | solution.py:74
  131.9 4.1 %multiply_reduce_fusion.2 = f32[4096]{0:T(1024)S(1)} fusion(bf16[4096,768]{1,0:T(8,128)(2,1)} %all-gather.8.cloned.1.call-done), kind=kLoop, calls=%fused_computation.4 | loop fusion | flops 9433088 | bytes 6307840 | tf_op jit(solution)/shard_map/reduce_sum | solution.py:10
  136.0 40.7 %all-gather.10.cloned.1.call-done = bf16[4096,768]{1,0:T(8,128)(2,1)} async-done(((bf16[256,768]{1,0:T(8,128)(2,1)}), bf16[4096,768]{1,0:T(8,128)(2,1)}) %all-gather.10.cloned.1.call-update) | async-done | bytes 6291472 | tf_op jit(solution)/shard_map/all_gather | solution.py:74
  176.7 4.2 %multiply_reduce_fusion.1 = f32[4096]{0:T(1024)S(1)} fusion(bf16[4096,768]{1,0:T(8,128)(2,1)} %all-gather.10.cloned.1.call-done), kind=kLoop, calls=%fused_computation.3 | loop fusion | flops 9433088 | bytes 6307840 | tf_op jit(solution)/shard_map/reduce_sum | solution.py:10
  181.3 4.2 %exponential_reduce_fusion.1 = f32[512]{0:T(512)S(1)} fusion(bf16[512,768]{1,0:T(8,128)(2,1)S(1)} %bitcast.71, bf16[4096,768]{1,0:T(8,128)(2,1)S(1)} %copy-done.1, f32[4096]{0:T(1024)S(1)} %multiply_reduce_fusion.2, f32[512]{0:T(512)S(1)} %bitcast.73), kind=kOutput, calls=%fused_computation.6 | convolution fusion | flops 3231710720 | bytes 7098368 | tf_op jit(solution)/shard_map/dot_general | solution.py:75
  185.5 4.2 %exponential_reduce_fusion = f32[512]{0:T(512)S(1)} fusion(bf16[512,768]{1,0:T(8,128)(2,1)S(1)} %bitcast.72, bf16[4096,768]{1,0:T(8,128)(2,1)S(1)} %bitcast.66, f32[4096]{0:T(1024)S(1)} %multiply_reduce_fusion.1, f32[512]{0:T(512)S(1)} %bitcast.74), kind=kOutput, calls=%fused_computation.5 | convolution fusion | flops 3231710720 | bytes 7098368 | tf_op jit(solution)/shard_map/dot_general | solution.py:75
  189.7 31.8 %all-gather.12.cloned.1.call-done = bf16[4096,768]{1,0:T(8,128)(2,1)} async-done(((bf16[256,768]{1,0:T(8,128)(2,1)}), bf16[4096,768]{1,0:T(8,128)(2,1)}) %all-gather.12.cloned.1.call-update) | async-done | bytes 6291472 | tf_op jit(solution)/shard_map/all_gather | solution.py:74
  221.4 4.2 %multiply_reduce_fusion = f32[4096]{0:T(1024)S(1)} fusion(bf16[4096,768]{1,0:T(8,128)(2,1)} %all-gather.12.cloned.1.call-done), kind=kLoop, calls=%fused_computation.2 | loop fusion | flops 9433088 | bytes 6307840 | tf_op jit(solution)/shard_map/reduce_sum | solution.py:10
  226.0 2.1 fusion.31
  229.0 1.3 collective-permute-start.1
  232.0 0.8 collective-permute-done.1
  234.8 4.1 %collective-permute-start.3 = (f32[]{:T(128)}, f32[]{:T(128)}, u32[]{:S(2)}, u32[]{:S(2)}) collective-permute-start(f32[]{:T(128)} %add.156), channel_id=1, source_target_pairs={{0,4},{1,5},{2,6},{3,7},{4,0},{5,1},{6,2},{7,3},{8,12},{9,13},{10,... | collective-permute-start | bytes 20 | tf_op jit(solution)/shard_map/ppermute | solution.py:49
  238.9 2.1 collective-permute-start.4
  241.0 2.8 collective-permute-start.5
  244.4 2.6 collective-permute-done.5
  248.2 4.1 %collective-permute-start.6 = (f32[]{:T(128)}, f32[]{:T(128)}, u32[]{:S(2)}, u32[]{:S(2)}) collective-permute-start(f32[]{:T(128)} %add.159), channel_id=1, source_target_pairs={{0,16},{16,0},{32,48},{48,32},{64,80},{80,64},{96,112},{112,96},{1... | collective-permute-start | bytes 20 | tf_op jit(solution)/shard_map/ppermute | solution.py:49
  252.3 2.8 %collective-permute-start.7 = (f32[]{:T(128)}, f32[]{:T(128)}, u32[]{:S(2)}, u32[]{:S(2)}) collective-permute-start(f32[]{:T(128)} %add.159), channel_id=1, source_target_pairs={{0,32},{16,48},{32,0},{48,16},{64,96},{80,112},{96,64},{112,80},{1... | collective-permute-start | bytes 20 | tf_op jit(solution)/shard_map/ppermute | solution.py:49
  255.1 2.1 collective-permute-start.8
  257.9 3.3 %collective-permute-done.8 = f32[]{:T(128)} collective-permute-done((f32[]{:T(128)}, f32[]{:T(128)}, u32[]{:S(2)}, u32[]{:S(2)}) %collective-permute-start.8) | collective-permute-done | bytes 36 | tf_op jit(solution)/shard_map/ppermute | solution.py:49
  262.4 4.1 %collective-permute-start.9 = (f32[]{:T(128)}, f32[]{:T(128)}, u32[]{:S(2)}, u32[]{:S(2)}) collective-permute-start(f32[]{:T(128)} %add.162), channel_id=1, source_target_pairs={{0,64},{16,80},{32,96},{48,112},{64,0},{80,16},{96,32},{112,48},{1... | collective-permute-start | bytes 20 | tf_op jit(solution)/shard_map/ppermute | solution.py:54
  266.5 1.0 collective-permute-done.9
  (50 shorter events, 8.0 us)
Async XLA Ops:
  6.5 1.6 copy-start
  6.5 44.1 %all-gather.16.cloned.1.call-start = ((), (), s32[]{:S(2)}) async-start(), calls=%async_computation.4 | async-start | bytes 3342336 | tf_op jit(solution)/shard_map/all_gather | solution.py:74
  12.4 75.4 %all-gather.14.cloned.1.call-start = ((), (), s32[]{:S(2)}) async-start(), calls=%async_computation.3 | async-start | bytes 3342336 | tf_op jit(solution)/shard_map/all_gather | solution.py:74
  13.1 118.7 %all-gather.8.cloned.1.call-start = ((), (), s32[]{:S(2)}) async-start(), calls=%async_computation | async-start | bytes 6684672 | tf_op jit(solution)/shard_map/all_gather | solution.py:74
  14.2 162.4 %all-gather.10.cloned.1.call-start = ((), (), s32[]{:S(2)}) async-start(), calls=%async_computation.1 | async-start | bytes 6684672 | tf_op jit(solution)/shard_map/all_gather | solution.py:74
  14.8 206.6 %all-gather.12.cloned.1.call-start = ((), (), s32[]{:S(2)}) async-start(), calls=%async_computation.2 | async-start | bytes 6684672 | tf_op jit(solution)/shard_map/all_gather | solution.py:74
  87.8 5.9 %copy-start.3 = (bf16[1,2048,768]{2,1,0:T(8,128)(2,1)S(1)}, bf16[1,2048,768]{2,1,0:T(8,128)(2,1)}, u32[]{:S(2)}) copy-start(bf16[1,2048,768]{2,1,0:T(8,128)(2,1)} %all-gather.14.cloned.1.call-done) | copy-start | bytes 9437188
  94.9 86.0 %copy-start.5 = (bf16[4,128,768]{2,1,0:T(8,128)(2,1)S(1)}, bf16[4,128,768]{2,1,0:T(8,128)(2,1)}, u32[]{:S(2)}) copy-start(bf16[4,128,768]{2,1,0:T(8,128)(2,1)} %slice.31) | copy-start | bytes 2359300
  176.7 4.6 %copy-start.1 = (bf16[4096,768]{1,0:T(8,128)(2,1)S(1)}, bf16[4096,768]{1,0:T(8,128)(2,1)}, u32[]{:S(2)}) copy-start(bf16[4096,768]{1,0:T(8,128)(2,1)} %all-gather.8.cloned.1.call-done) | copy-start | bytes 18874372
  176.7 8.8 %slice-start = ((s8[6291456]{0:T(1024)(128)(4,1)}), s8[4194304]{0:T(1024)(128)(4,1)S(1)}, s32[]{:S(2)}) async-start(s8[6291456]{0:T(1024)(128)(4,1)} %bitcast.65), calls=%async_computation.5 | async-start | bytes 8388608
  181.3 4.2 %slice-start.1 = ((s8[6291456]{0:T(1024)(128)(4,1)}), s8[2097152]{0:T(1024)(128)(4,1)S(1)}, s32[]{:S(2)}) async-start(s8[6291456]{0:T(1024)(128)(4,1)} %bitcast.65), calls=%async_computation.6 | async-start | bytes 4194304
  185.5 40.2 %copy-start.4 = (bf16[2,128,768]{2,1,0:T(8,128)(2,1)S(1)}, bf16[2,128,768]{2,1,0:T(8,128)(2,1)}, u32[]{:S(2)}) copy-start(bf16[2,128,768]{2,1,0:T(8,128)(2,1)} %get-tuple-element.10) | copy-start | bytes 1179652
  221.4 4.6 %copy-start.2 = (bf16[4096,768]{1,0:T(8,128)(2,1)S(1)}, bf16[4096,768]{1,0:T(8,128)(2,1)}, u32[]{:S(2)}) copy-start(bf16[4096,768]{1,0:T(8,128)(2,1)} %all-gather.12.cloned.1.call-done) | copy-start | bytes 18874372
  228.8 1.9 collective-permute-start
  229.0 3.8 %collective-permute-start.1 = (f32[]{:T(128)}, f32[]{:T(128)}, u32[]{:S(2)}, u32[]{:S(2)}) collective-permute-start(f32[]{:T(128)} %fusion.43), channel_id=1, source_target_pairs={{0,2},{1,3},{2,0},{3,1},{4,6},{5,7},{6,4},{7,5},{8,10},{9,11},{10,... | collective-permute-start | bytes 20 | tf_op jit(solution)/shard_map/ppermute | solution.py:49
  230.3 3.2 %collective-permute-start.2 = (f32[]{:T(128)}, f32[]{:T(128)}, u32[]{:S(2)}, u32[]{:S(2)}) collective-permute-start(f32[]{:T(128)} %fusion.43), channel_id=1, source_target_pairs={{0,3},{1,2},{2,1},{3,0},{4,7},{5,6},{6,5},{7,4},{8,11},{9,10},{10,... | collective-permute-start | bytes 20 | tf_op jit(solution)/shard_map/ppermute | solution.py:49
  234.8 9.0 %collective-permute-start.3 = (f32[]{:T(128)}, f32[]{:T(128)}, u32[]{:S(2)}, u32[]{:S(2)}) collective-permute-start(f32[]{:T(128)} %add.156), channel_id=1, source_target_pairs={{0,4},{1,5},{2,6},{3,7},{4,0},{5,1},{6,2},{7,3},{8,12},{9,13},{10,... | collective-permute-start | bytes 20 | tf_op jit(solution)/shard_map/ppermute | solution.py:49
  238.9 5.5 %collective-permute-start.4 = (f32[]{:T(128)}, f32[]{:T(128)}, u32[]{:S(2)}, u32[]{:S(2)}) collective-permute-start(f32[]{:T(128)} %add.156), channel_id=1, source_target_pairs={{0,8},{1,9},{2,10},{3,11},{4,12},{5,13},{6,14},{7,15},{8,0},{9,1},... | collective-permute-start | bytes 20 | tf_op jit(solution)/shard_map/ppermute | solution.py:49
  241.0 6.1 %collective-permute-start.5 = (f32[]{:T(128)}, f32[]{:T(128)}, u32[]{:S(2)}, u32[]{:S(2)}) collective-permute-start(f32[]{:T(128)} %add.156), channel_id=1, source_target_pairs={{0,12},{1,13},{2,14},{3,15},{4,8},{5,9},{6,10},{7,11},{8,4},{9,5},... | collective-permute-start | bytes 20 | tf_op jit(solution)/shard_map/ppermute | solution.py:49
  248.2 9.0 %collective-permute-start.6 = (f32[]{:T(128)}, f32[]{:T(128)}, u32[]{:S(2)}, u32[]{:S(2)}) collective-permute-start(f32[]{:T(128)} %add.159), channel_id=1, source_target_pairs={{0,16},{16,0},{32,48},{48,32},{64,80},{80,64},{96,112},{112,96},{1... | collective-permute-start | bytes 20 | tf_op jit(solution)/shard_map/ppermute | solution.py:49
  252.3 5.6 %collective-permute-start.7 = (f32[]{:T(128)}, f32[]{:T(128)}, u32[]{:S(2)}, u32[]{:S(2)}) collective-permute-start(f32[]{:T(128)} %add.159), channel_id=1, source_target_pairs={{0,32},{16,48},{32,0},{48,16},{64,96},{80,112},{96,64},{112,80},{1... | collective-permute-start | bytes 20 | tf_op jit(solution)/shard_map/ppermute | solution.py:49
  255.1 6.1 %collective-permute-start.8 = (f32[]{:T(128)}, f32[]{:T(128)}, u32[]{:S(2)}, u32[]{:S(2)}) collective-permute-start(f32[]{:T(128)} %add.159), channel_id=1, source_target_pairs={{0,48},{16,32},{32,16},{48,0},{64,112},{80,96},{96,80},{112,64},{1... | collective-permute-start | bytes 20 | tf_op jit(solution)/shard_map/ppermute | solution.py:49
  262.4 5.1 %collective-permute-start.9 = (f32[]{:T(128)}, f32[]{:T(128)}, u32[]{:S(2)}, u32[]{:S(2)}) collective-permute-start(f32[]{:T(128)} %add.162), channel_id=1, source_target_pairs={{0,64},{16,80},{32,96},{48,112},{64,0},{80,16},{96,32},{112,48},{1... | collective-permute-start | bytes 20 | tf_op jit(solution)/shard_map/ppermute | solution.py:54
Sparse Core Ops, SparseCore 0:
  12.5 38.0 all-gather.15
  52.3 35.4 all-gather.13
  89.5 42.3 all-gather.7
  133.4 43.1 all-gather.9
  178.2 43.1 all-gather.11

commit v2 on v1

v2 whole, which is shorter than its diff:
```python
import itertools

import jax
import jax.numpy as jnp
from jax import lax
from jax.sharding import PartitionSpec as P

BLK = 128


def squared(values):
    return jnp.sum(jnp.square(values.astype(jnp.float32)), axis=1)


def class_spans(count):
    spans = []
    start = 0
    width = count // 2
    while start < count:
        end = min(start + max(width, 1), count)
        spans.append((start, end))
        start = end
        width //= 2
    return spans


def member_ring(count):
    if count != 16:
        return list(range(count))
    chips = [(0, 0), (0, 1), (0, 2), (0, 3), (1, 3), (1, 2), (1, 1), (1, 0)]
    return [x * 8 + z * 2 + core for x, z in chips for core in (0, 1)]


def cover(count):
    best = None
    half = count // 2
    for size in range(2, count + 1):
        for rest in itertools.combinations(range(1, count), size - 1):
            offsets = (0,) + rest
            kinds = set()
            for a, b in itertools.combinations(offsets, 2):
                step = (b - a) % count
                kinds.add(min(step, count - step))
            if kinds >= set(range(1, half + 1)):
                cost = sum(min(d, count - d) for d in rest)
                if best is None or cost < best[0]:
                    best = (cost, offsets)
        if best is not None:
            return best[1]
    return tuple(range(count))


def plan(count):
    offsets = cover(count)
    pairs = []
    for step in range(1, count // 2 + 1):
        for a, b in itertools.permutations(offsets, 2):
            if (b - a) % count == step:
                pairs.append((a, b, 2 * step != count))
                break
    return offsets, pairs


def tree_total(value, axis, size):
    stride = 1
    while stride < size:
        value = value + lax.ppermute(value, axis, [(i, i ^ stride) for i in range(size)])
        stride *= 2
    return value


def kernel_sums(left, right, left_norms, right_norms, both):
    products = lax.dot_general(
        left, right, (((1,), (1,)), ((), ())), preferred_element_type=jnp.float32
    )
    distance = left_norms[:, None] + right_norms[None, :] - 2.0 * products
    kernel = jnp.exp(-0.5 * distance)
    rows = jnp.sum(kernel, axis=1)
    cols = jnp.sum(kernel, axis=0) if both else None
    return rows, cols


def shards(embeddings, block_order):
    row_count, width = embeddings.shape
    member_count = lax.axis_size("mem")
    position = lax.axis_index("mem")
    per_device = row_count // BLK
    order = lax.dynamic_slice_in_dim(block_order[0], position * per_device, per_device)
    blocks = embeddings.reshape(per_device, BLK, width)
    ordered = jnp.take(blocks, order, axis=0).reshape(row_count, width)
    spans = [(start * BLK, end * BLK) for start, end in class_spans(per_device)]

    ring = member_ring(member_count)
    offsets, pairs = plan(member_count)

    def fetch(value, offset):
        return lax.ppermute(
            value,
            "mem",
            [(ring[(r + offset) % member_count], ring[r]) for r in range(member_count)],
        )

    def give_back(value, offset):
        return lax.ppermute(
            value,
            "mem",
            [(ring[r], ring[(r + offset) % member_count]) for r in range(member_count)],
        )

    held = {0: ordered}
    for offset in offsets[1:]:
        held[offset] = fetch(ordered, offset)
    norms = {offset: squared(rows) for offset, rows in held.items()}
    partial = {offset: [None] * len(spans) for offset in offsets}

    def add(offset, index, value):
        slot = partial[offset]
        slot[index] = value if slot[index] is None else slot[index] + value

    for index, (start, end) in enumerate(spans):
        own = held[0][start:end]
        own_norms = norms[0][start:end]
        rows, _ = kernel_sums(own, own, own_norms, own_norms, False)
        add(0, index, rows)
        for a, b, both in pairs:
            rows, cols = kernel_sums(
                held[a][start:end], held[b][start:end],
                norms[a][start:end], norms[b][start:end], both,
            )
            add(a, index, rows)
            if both:
                add(b, index, cols)

    gathered = {}
    for offset in offsets:
        parts = [
            value if value is not None else jnp.zeros((end - start,), jnp.float32)
            for value, (start, end) in zip(partial[offset], spans)
        ]
        gathered[offset] = jnp.concatenate(parts)
    density = gathered[0]
    for offset in offsets[1:]:
        density = density + give_back(gathered[offset], offset)

    inverse = 1.0 / density.reshape(per_device, BLK)
    total = tree_total(jnp.sum(inverse), "mem", member_count)
    total = tree_total(total, "clu", lax.axis_size("clu"))
    everything = jnp.float32(row_count * lax.axis_size("clu") * member_count)
    weight = inverse * (everything / total)
    spots = jnp.arange(per_device, dtype=jnp.int32)
    back = jnp.sum(
        jnp.where(order[None, :] == spots[:, None], spots[None, :], 0), axis=1
    )
    return jnp.take(weight, back, axis=0).reshape(-1)


def solution(mesh):
    placed = (P(("clu", "mem"), None), P("clu", None))
    return jax.shard_map(
        shards, mesh=mesh, in_specs=placed, out_specs=P(("clu", "mem")), check_vma=False
    )
```

time: 276 us -> 150 us (0.54)
  waiting for transfers between devices: 188 us -> 88.6 us
  other arithmetic: 23 us -> 5.54 us
  between operations: 20.4 us -> 6.14 us
  starting transfers between devices: 24 us -> 33.2 us
  local copies, waits for them, and re-layouts: 5.91 us -> 1.5 us
    all_gather x5 -> x0, waiting for transfers between devices: 177 us -> none  [shards(): lax.all_gather(ordered[start:stop].reshape(-1, width), 'mem', axis=0, til...]
    ppermute x9 -> x8, waiting for transfers between devices: 7.43 us -> 81.7 us  [the longest x4 78.8 us: fetch(): lax.ppermute(value, 'mem', [(ring[(r + offset) % member_count], ring[r])...]
    ppermute x1 -> x7, starting transfers between devices: 4.1 us -> 20.6 us  [tree_total(): lax.ppermute(value, axis, [(i, i ^ stride) for i in range(size)])]
    reduce_sum x8 -> x5, other arithmetic: 18.4 us -> 2.09 us  [squared(): return jnp.sum(jnp.square(values.astype(jnp.float32)), axis=1)]
    ppermute x9 -> x8, starting transfers between devices: 19.8 us -> 12.6 us  [the longest x4 6.56 us: give_back(): lax.ppermute(value, 'mem', [(ring[r], ring[(r + offset) % member_count])...]
    ppermute x1 -> x7, waiting for transfers between devices: 1 us -> 6.87 us  [tree_total(): lax.ppermute(value, axis, [(i, i ^ stride) for i in range(size)])]
    dot_general x5 -> x36, matrix products: 14.9 us -> 14.9 us  [kernel_sums(): lax.dot_general(left, right, (((1,), (1,)), ((), ())), preferred_element_...]
  transfers between devices with their start and end apart: 15 -> 15, of which waited for: 10 -> 11; matrix products, arithmetic and copies ran while one was open for 11% -> 4% of each run, Pallas kernels for 0% -> 0%
where the time goes in v2:
time: 150 us
  waiting for transfers between devices  88.6 us (59%)
  starting transfers between devices  33.2 us (22%)
  matrix products  14.9 us (10%)
  between operations  6.14 us (4%)
  other arithmetic  5.54 us (4%)
  local copies, waits for them, and re-layouts  1.5 us (1%)
    ppermute x4, waiting for transfers between devices, fetch(): lax.ppermute(value, 'mem', [(ring[(r + offset) % member_count], ring[r])...  78.8 us
    ppermute x7, starting transfers between devices, tree_total(): lax.ppermute(value, axis, [(i, i ^ stride) for i in range(size)])  20.6 us
    dot_general x36, matrix products, kernel_sums(): lax.dot_general(left, right, (((1,), (1,)), ((), ())), preferred_element_...  14.9 us
    ppermute x7, waiting for transfers between devices, tree_total(): lax.ppermute(value, axis, [(i, i ^ stride) for i in range(size)])  6.87 us
    ppermute x4, starting transfers between devices, give_back(): lax.ppermute(value, 'mem', [(ring[r], ring[(r + offset) % member_count])...  6.56 us
    ppermute x4, starting transfers between devices, fetch(): lax.ppermute(value, 'mem', [(ring[(r + offset) % member_count], ring[r])...  6.08 us
  transfers between devices with their start and end apart: 15, of which 11 were waited for; matrix products, arithmetic and copies ran while one was open for 4% of the time, Pallas kernels for 0%

profile of v2, /device:TPU:0, one launch (start us, length us, event | category | flops | bytes accessed | tf_op | source)
XLA Modules:
  0.0 150.0 jit_solution(11397044260741460396)
XLA Ops:
  0.0 0.8 fusion.146
  0.9 0.7 compare_and_fusion
  1.7 0.6 gather_fusion
  2.6 1.1 collective-permute-start
  3.7 1.9 %collective-permute-start.1 = (bf16[1024,768]{1,0:T(8,128)(2,1)S(1)}, bf16[1024,768]{1,0:T(8,128)(2,1)S(1)}, u32[]{:S(2)}, u32[]{:S(2)}) collective-permute-start(bf16[1024,768]{1,0:T(8,128)(2,1)S(1)} %bitcast_select_fusion), channel_id=1, source_target_pairs={{2,0},{3,1},{4,2},{5,3},{6,4},{7,5},{14,6},{15,7},{12,14},{13,15},... | collective-permute-start | bytes 4718600 | tf_op jit(solution)/shard_map/ppermute | solution.py:97
  5.7 3.0 %collective-permute-start.2 = (bf16[1024,768]{1,0:T(8,128)(2,1)S(1)}, bf16[1024,768]{1,0:T(8,128)(2,1)S(1)}, u32[]{:S(2)}, u32[]{:S(2)}) collective-permute-start(bf16[1024,768]{1,0:T(8,128)(2,1)S(1)} %bitcast_select_fusion), channel_id=1, source_target_pairs={{12,0},{13,1},{10,2},{11,3},{8,4},{9,5},{0,6},{1,7},{2,14},{3,15},... | collective-permute-start | bytes 4718600 | tf_op jit(solution)/shard_map/ppermute | solution.py:97
  10.5 0.7 fusion.3
  11.2 27.3 %collective-permute-done = bf16[1024,768]{1,0:T(8,128)(2,1)S(1)} collective-permute-done((bf16[1024,768]{1,0:T(8,128)(2,1)S(1)}, bf16[1024,768]{1,0:T(8,128)(2,1)S(1)}, u32[]{:S(2)}, u32[]{:S(2)}) %collective-permute-start) | collective-permute-done | bytes 1572896 | tf_op jit(solution)/shard_map/ppermute | solution.py:97
  38.8 51.5 %collective-permute-done.1 = bf16[1024,768]{1,0:T(8,128)(2,1)S(1)} collective-permute-done((bf16[1024,768]{1,0:T(8,128)(2,1)S(1)}, bf16[1024,768]{1,0:T(8,128)(2,1)S(1)}, u32[]{:S(2)}, u32[]{:S(2)}) %collective-permute-start.1) | collective-permute-done | bytes 1572896 | tf_op jit(solution)/shard_map/ppermute | solution.py:97
  93.5 0.6 convolution_multiply_fusion.6
  94.7 0.6 convolution_multiply_fusion.4
  96.0 0.6 convolution_multiply_fusion.5
  96.6 0.6 convolution_multiply_fusion.3
  97.3 2.2 %fusion.17 = (f32[512]{0:T(512)S(1)}, f32[512]{0:T(512)S(1)}, f32[512]{0:T(512)S(1)}, f32[512]{0:T(512)S(1)}, f32[512]{0:T(512)S(1)}, /*index=5*/f32[512]{0:T(51...) fusion(f32[512]{0:T(512)S(1)} %slice-done, ...), kind=kOutput, calls=%fused_computation.70 | convolution fusion | flops 412083200 | bytes 7907328 | tf_op jit(solution)/shard_map/dot_general | solution.py:73
  104.1 3.6 %collective-permute-start.6 = (f32[1024]{0:T(1024)S(1)}, f32[1024]{0:T(1024)S(1)}, u32[]{:S(2)}, u32[]{:S(2)}) collective-permute-start(f32[1024]{0:T(1024)S(1)} %pad_maximum_fusion.2), channel_id=1, source_target_pairs={{0,12},{1,13},{2,10},{3,11},{4,8},{5,9},{6,0},{7,1},{14,2},{15,3},... | collective-permute-start | bytes 12296 | tf_op jit(solution)/shard_map/ppermute | solution.py:104
  108.1 0.7 exponential_reduce_fusion
  109.4 2.6 %collective-permute-start.5 = (f32[1024]{0:T(1024)S(1)}, f32[1024]{0:T(1024)S(1)}, u32[]{:S(2)}, u32[]{:S(2)}) collective-permute-start(f32[1024]{0:T(1024)S(1)} %pad_maximum_fusion.1), channel_id=1, source_target_pairs={{0,2},{1,3},{2,4},{3,5},{4,6},{5,7},{6,14},{7,15},{14,12},{15,13},... | collective-permute-start | bytes 12296 | tf_op jit(solution)/shard_map/ppermute | solution.py:104
  112.1 1.1 collective-permute-done.5
  113.3 1.8 %collective-permute-done.4 = f32[1024]{0:T(1024)S(1)} collective-permute-done((f32[1024]{0:T(1024)S(1)}, f32[1024]{0:T(1024)S(1)}, u32[]{:S(2)}, u32[]{:S(2)}) %collective-permute-start.4) | collective-permute-done | bytes 4128 | tf_op jit(solution)/shard_map/ppermute | solution.py:104
  115.1 0.6 fusion.152
  115.7 1.3 collective-permute-done.8
  118.3 3.5 %collective-permute-start.9 = (f32[]{:T(128)}, f32[]{:T(128)}, u32[]{:S(2)}, u32[]{:S(2)}) collective-permute-start(f32[]{:T(128)} %add.730), channel_id=1, source_target_pairs={{0,2},{1,3},{2,0},{3,1},{4,6},{5,7},{6,4},{7,5},{8,10},{9,11},{10,... | collective-permute-start | bytes 20 | tf_op jit(solution)/shard_map/ppermute | solution.py:67
  122.7 3.9 %collective-permute-start.10 = (f32[]{:T(128)}, f32[]{:T(128)}, u32[]{:S(2)}, u32[]{:S(2)}) collective-permute-start(f32[]{:T(128)} %add.731), channel_id=1, source_target_pairs={{0,4},{1,5},{2,6},{3,7},{4,0},{5,1},{6,2},{7,3},{8,12},{9,13},{10,... | collective-permute-start | bytes 20 | tf_op jit(solution)/shard_map/ppermute | solution.py:67
  126.6 1.2 collective-permute-done.10
  128.5 1.7 %collective-permute-start.11 = (f32[]{:T(128)}, f32[]{:T(128)}, u32[]{:S(2)}, u32[]{:S(2)}) collective-permute-start(f32[]{:T(128)} %add.732), channel_id=1, source_target_pairs={{0,8},{1,9},{2,10},{3,11},{4,12},{5,13},{6,14},{7,15},{8,0},{9,1},... | collective-permute-start | bytes 20 | tf_op jit(solution)/shard_map/ppermute | solution.py:67
  130.2 1.9 %collective-permute-done.11 = f32[]{:T(128)} collective-permute-done((f32[]{:T(128)}, f32[]{:T(128)}, u32[]{:S(2)}, u32[]{:S(2)}) %collective-permute-start.11) | collective-permute-done | bytes 36 | tf_op jit(solution)/shard_map/ppermute | solution.py:67
  132.8 4.0 %collective-permute-start.12 = (f32[]{:T(128)}, f32[]{:T(128)}, u32[]{:S(2)}, u32[]{:S(2)}) collective-permute-start(f32[]{:T(128)} %add.733), channel_id=1, source_target_pairs={{0,16},{16,0},{32,48},{48,32},{64,80},{80,64},{96,112},{112,96},{1... | collective-permute-start | bytes 20 | tf_op jit(solution)/shard_map/ppermute | solution.py:67
  136.8 1.1 collective-permute-done.12
  138.6 3.0 %collective-permute-start.13 = (f32[]{:T(128)}, f32[]{:T(128)}, u32[]{:S(2)}, u32[]{:S(2)}) collective-permute-start(f32[]{:T(128)} %add.734), channel_id=1, source_target_pairs={{0,32},{16,48},{32,0},{48,16},{64,96},{80,112},{96,64},{112,80},{1... | collective-permute-start | bytes 20 | tf_op jit(solution)/shard_map/ppermute | solution.py:67
  141.5 0.6 collective-permute-done.13
  142.9 4.6 %collective-permute-start.14 = (f32[]{:T(128)}, f32[]{:T(128)}, u32[]{:S(2)}, u32[]{:S(2)}) collective-permute-start(f32[]{:T(128)} %add.735), channel_id=1, source_target_pairs={{0,64},{16,80},{32,96},{48,112},{64,0},{80,16},{96,32},{112,48},{1... | collective-permute-start | bytes 20 | tf_op jit(solution)/shard_map/ppermute | solution.py:67
  149.3 0.7 select_bitcast_fusion
  (97 shorter events, 13.5 us)
Async XLA Ops:
  0.0 1.7 %copy-start = (bf16[1024,768]{1,0:T(8,128)(2,1)S(1)}, bf16[1024,768]{1,0:T(8,128)(2,1)}, u32[]{:S(2)}) copy-start(bf16[1024,768]{1,0:T(8,128)(2,1)} %param.2) | copy-start | bytes 4718596
  2.6 35.8 %collective-permute-start = (bf16[1024,768]{1,0:T(8,128)(2,1)S(1)}, bf16[1024,768]{1,0:T(8,128)(2,1)S(1)}, u32[]{:S(2)}, u32[]{:S(2)}) collective-permute-start(bf16[1024,768]{1,0:T(8,128)(2,1)S(1)} %bitcast_select_fusion), channel_id=1, source_target_pairs={{1,0},{2,1},{3,2},{4,3},{5,4},{6,5},{7,6},{14,7},{15,14},{12,15},{... | collective-permute-start | bytes 4718600 | tf_op jit(solution)/shard_map/ppermute | solution.py:97
  3.7 86.6 %collective-permute-start.1 = (bf16[1024,768]{1,0:T(8,128)(2,1)S(1)}, bf16[1024,768]{1,0:T(8,128)(2,1)S(1)}, u32[]{:S(2)}, u32[]{:S(2)}) collective-permute-start(bf16[1024,768]{1,0:T(8,128)(2,1)S(1)} %bitcast_select_fusion), channel_id=1, source_target_pairs={{2,0},{3,1},{4,2},{5,3},{6,4},{7,5},{14,6},{15,7},{12,14},{13,15},... | collective-permute-start | bytes 4718600 | tf_op jit(solution)/shard_map/ppermute | solution.py:97
  5.7 85.1 %collective-permute-start.3 = (bf16[1024,768]{1,0:T(8,128)(2,1)S(1)}, bf16[1024,768]{1,0:T(8,128)(2,1)S(1)}, u32[]{:S(2)}, u32[]{:S(2)}) collective-permute-start(bf16[1024,768]{1,0:T(8,128)(2,1)S(1)} %bitcast_select_fusion), channel_id=1, source_target_pairs={{11,0},{8,1},{9,2},{0,3},{1,4},{2,5},{3,6},{4,7},{5,14},{6,15},{7,... | collective-permute-start | bytes 4718600 | tf_op jit(solution)/shard_map/ppermute | solution.py:97
  5.7 85.5 %collective-permute-start.2 = (bf16[1024,768]{1,0:T(8,128)(2,1)S(1)}, bf16[1024,768]{1,0:T(8,128)(2,1)S(1)}, u32[]{:S(2)}, u32[]{:S(2)}) collective-permute-start(bf16[1024,768]{1,0:T(8,128)(2,1)S(1)} %bitcast_select_fusion), channel_id=1, source_target_pairs={{12,0},{13,1},{10,2},{11,3},{8,4},{9,5},{0,6},{1,7},{2,14},{3,15},... | collective-permute-start | bytes 4718600 | tf_op jit(solution)/shard_map/ppermute | solution.py:97
  38.8 52.8 %copy-start.1 = (f32[1024]{0:T(1024)}, f32[1024]{0:T(1024)S(1)}, u32[]{:S(2)}) copy-start(f32[1024]{0:T(1024)S(1)} %multiply_reduce_fusion.3) | copy-start | bytes 12292
  91.1 1.1 copy-start.2
  96.6 0.7 slice-start
  96.6 0.7 slice-start.1
  102.9 9.2 %collective-permute-start.7 = (f32[1024]{0:T(1024)S(1)}, f32[1024]{0:T(1024)S(1)}, u32[]{:S(2)}, u32[]{:S(2)}) collective-permute-start(f32[1024]{0:T(1024)S(1)} %pad_maximum_fusion.3), channel_id=1, source_target_pairs={{0,11},{1,8},{2,9},{3,0},{4,1},{5,2},{6,3},{7,4},{14,5},{15,6},{12... | collective-permute-start | bytes 12296 | tf_op jit(solution)/shard_map/ppermute | solution.py:104
  104.1 8.0 %collective-permute-start.6 = (f32[1024]{0:T(1024)S(1)}, f32[1024]{0:T(1024)S(1)}, u32[]{:S(2)}, u32[]{:S(2)}) collective-permute-start(f32[1024]{0:T(1024)S(1)} %pad_maximum_fusion.2), channel_id=1, source_target_pairs={{0,12},{1,13},{2,10},{3,11},{4,8},{5,9},{6,0},{7,1},{14,2},{15,3},... | collective-permute-start | bytes 12296 | tf_op jit(solution)/shard_map/ppermute | solution.py:104
  109.4 3.9 %collective-permute-start.5 = (f32[1024]{0:T(1024)S(1)}, f32[1024]{0:T(1024)S(1)}, u32[]{:S(2)}, u32[]{:S(2)}) collective-permute-start(f32[1024]{0:T(1024)S(1)} %pad_maximum_fusion.1), channel_id=1, source_target_pairs={{0,2},{1,3},{2,4},{3,5},{4,6},{5,7},{6,14},{7,15},{14,12},{15,13},... | collective-permute-start | bytes 12296 | tf_op jit(solution)/shard_map/ppermute | solution.py:104
  112.0 3.1 %collective-permute-start.4 = (f32[1024]{0:T(1024)S(1)}, f32[1024]{0:T(1024)S(1)}, u32[]{:S(2)}, u32[]{:S(2)}) collective-permute-start(f32[1024]{0:T(1024)S(1)} %pad_maximum_fusion), channel_id=1, source_target_pairs={{0,1},{1,2},{2,3},{3,4},{4,5},{5,6},{6,7},{7,14},{14,15},{15,12},{... | collective-permute-start | bytes 12296 | tf_op jit(solution)/shard_map/ppermute | solution.py:104
  115.7 1.3 collective-permute-start.8
  118.3 3.7 %collective-permute-start.9 = (f32[]{:T(128)}, f32[]{:T(128)}, u32[]{:S(2)}, u32[]{:S(2)}) collective-permute-start(f32[]{:T(128)} %add.730), channel_id=1, source_target_pairs={{0,2},{1,3},{2,0},{3,1},{4,6},{5,7},{6,4},{7,5},{8,10},{9,11},{10,... | collective-permute-start | bytes 20 | tf_op jit(solution)/shard_map/ppermute | solution.py:67
  122.7 5.1 %collective-permute-start.10 = (f32[]{:T(128)}, f32[]{:T(128)}, u32[]{:S(2)}, u32[]{:S(2)}) collective-permute-start(f32[]{:T(128)} %add.731), channel_id=1, source_target_pairs={{0,4},{1,5},{2,6},{3,7},{4,0},{5,1},{6,2},{7,3},{8,12},{9,13},{10,... | collective-permute-start | bytes 20 | tf_op jit(solution)/shard_map/ppermute | solution.py:67
  128.5 3.6 %collective-permute-start.11 = (f32[]{:T(128)}, f32[]{:T(128)}, u32[]{:S(2)}, u32[]{:S(2)}) collective-permute-start(f32[]{:T(128)} %add.732), channel_id=1, source_target_pairs={{0,8},{1,9},{2,10},{3,11},{4,12},{5,13},{6,14},{7,15},{8,0},{9,1},... | collective-permute-start | bytes 20 | tf_op jit(solution)/shard_map/ppermute | solution.py:67
  132.8 5.1 %collective-permute-start.12 = (f32[]{:T(128)}, f32[]{:T(128)}, u32[]{:S(2)}, u32[]{:S(2)}) collective-permute-start(f32[]{:T(128)} %add.733), channel_id=1, source_target_pairs={{0,16},{16,0},{32,48},{48,32},{64,80},{80,64},{96,112},{112,96},{1... | collective-permute-start | bytes 20 | tf_op jit(solution)/shard_map/ppermute | solution.py:67
  138.6 3.6 %collective-permute-start.13 = (f32[]{:T(128)}, f32[]{:T(128)}, u32[]{:S(2)}, u32[]{:S(2)}) collective-permute-start(f32[]{:T(128)} %add.734), channel_id=1, source_target_pairs={{0,32},{16,48},{32,0},{48,16},{64,96},{80,112},{96,64},{112,80},{1... | collective-permute-start | bytes 20 | tf_op jit(solution)/shard_map/ppermute | solution.py:67
  142.9 5.1 %collective-permute-start.14 = (f32[]{:T(128)}, f32[]{:T(128)}, u32[]{:S(2)}, u32[]{:S(2)}) collective-permute-start(f32[]{:T(128)} %add.735), channel_id=1, source_target_pairs={{0,64},{16,80},{32,96},{48,112},{64,0},{80,16},{96,32},{112,48},{1... | collective-permute-start | bytes 20 | tf_op jit(solution)/shard_map/ppermute | solution.py:67

commit v3 on v2

--- a/solution.py
+++ b/solution.py
@@ -28,10 +28,12 @@
     if count != 16:
         return list(range(count))
     chips = [(0, 0), (0, 1), (0, 2), (0, 3), (1, 3), (1, 2), (1, 1), (1, 0)]
-    return [x * 8 + z * 2 + core for x, z in chips for core in (0, 1)]
+    return [x * 8 + z * 2 + core for core in (0, 1) for x, z in chips]
 
 
 def cover(count):
+    if count == 16:
+        return (0, 1, 5, 8, 15)
     best = None
     half = count // 2
     for size in range(2, count + 1):
@@ -61,12 +63,9 @@
     return offsets, pairs
 
 
-def tree_total(value, axis, size):
-    stride = 1
-    while stride < size:
-        value = value + lax.ppermute(value, axis, [(i, i ^ stride) for i in range(size)])
-        stride *= 2
-    return value
+def grand_total(value, axes, size):
+    spread = lax.all_to_all(jnp.broadcast_to(value, (size, 1)), axes, 0, 0, tiled=True)
+    return jnp.sum(spread)
 
 
 def kernel_sums(left, right, left_norms, right_norms, both):
@@ -143,8 +142,7 @@
         density = density + give_back(gathered[offset], offset)
 
     inverse = 1.0 / density.reshape(per_device, BLK)
-    total = tree_total(jnp.sum(inverse), "mem", member_count)
-    total = tree_total(total, "clu", lax.axis_size("clu"))
+    total = grand_total(jnp.sum(inverse), ("clu", "mem"), lax.axis_size("clu") * member_count)
     everything = jnp.float32(row_count * lax.axis_size("clu") * member_count)
     weight = inverse * (everything / total)
     spots = jnp.arange(per_device, dtype=jnp.int32)

time: 150 us -> 121 us (0.81)
  waiting for transfers between devices: 88.6 us -> 73.7 us
  starting transfers between devices: 33.2 us -> 21.1 us
  between operations: 6.14 us -> 1.29 us
    ppermute x7 -> x0, starting transfers between devices: 20.6 us -> none  [tree_total(): lax.ppermute(value, axis, [(i, i ^ stride) for i in range(size)])]
    ppermute x4, waiting for transfers between devices: 78.8 us -> 62.8 us  [fetch(): lax.ppermute(value, 'mem', [(ring[(r + offset) % member_count], ring[r])...]
    all_to_all x0 -> x1, waiting for transfers between devices: none -> 9.53 us  [grand_total(): lax.all_to_all(jnp.broadcast_to(value, (size, 1)), axes, 0, 0, tiled=True)]
    all_to_all x0 -> x1, starting transfers between devices: none -> 8.25 us  [grand_total(): lax.all_to_all(jnp.broadcast_to(value, (size, 1)), axes, 0, 0, tiled=True)]
    ppermute x7 -> x0, waiting for transfers between devices: 6.87 us -> none  [tree_total(): lax.ppermute(value, axis, [(i, i ^ stride) for i in range(size)])]
    ppermute x4, waiting for transfers between devices: 2.96 us -> 1.39 us  [give_back(): lax.ppermute(value, 'mem', [(ring[r], ring[(r + offset) % member_count])...]
  transfers between devices with their start and end apart: 15 -> 9, of which waited for: 11 -> 5; matrix products, arithmetic and copies ran while one was open for 4% -> 6% of each run, Pallas kernels for 0% -> 0%
where the time goes in v3:
time: 121 us; the launch traced here: 120 us
  waiting for transfers between devices  73.7 us (61%)
  starting transfers between devices  21.1 us (17%)
  matrix products  15.3 us (13%)
  other arithmetic  6.29 us (5%)
  local copies, waits for them, and re-layouts  2.79 us (2%)
  between operations  1.29 us (1%)
    ppermute x4, waiting for transfers between devices, fetch(): lax.ppermute(value, 'mem', [(ring[(r + offset) % member_count], ring[r])...  62.8 us
    dot_general x36, matrix products, kernel_sums(): lax.dot_general(left, right, (((1,), (1,)), ((), ())), preferred_element_...  15.3 us
    all_to_all x1, waiting for transfers between devices, grand_total(): lax.all_to_all(jnp.broadcast_to(value, (size, 1)), axes, 0, 0, tiled=True)  9.53 us
    all_to_all x1, starting transfers between devices, grand_total(): lax.all_to_all(jnp.broadcast_to(value, (size, 1)), axes, 0, 0, tiled=True)  8.25 us
    ppermute x4, starting transfers between devices, give_back(): lax.ppermute(value, 'mem', [(ring[r], ring[(r + offset) % member_count])...  6.51 us
    ppermute x4, starting transfers between devices, fetch(): lax.ppermute(value, 'mem', [(ring[(r + offset) % member_count], ring[r])...  6.37 us
  transfers between devices with their start and end apart: 9, of which 5 were waited for; matrix products, arithmetic and copies ran while one was open for 6% of the time, Pallas kernels for 0%

profile of v3, /device:TPU:0, one launch (start us, length us, event | category | flops | bytes accessed | tf_op | source)
XLA Modules:
  0.0 120.5 jit_solution(10569127373818537357)
XLA Ops:
  0.0 0.8 fusion.144
  0.9 0.7 compare_and_fusion
  1.7 0.6 gather_fusion
  2.6 1.1 collective-permute-start
  3.8 2.7 %collective-permute-start.1 = (bf16[1024,768]{1,0:T(8,128)(2,1)S(1)}, bf16[1024,768]{1,0:T(8,128)(2,1)S(1)}, u32[]{:S(2)}, u32[]{:S(2)}) collective-permute-start(bf16[1024,768]{1,0:T(8,128)(2,1)S(1)} %bitcast_select_fusion), channel_id=1, source_target_pairs={{12,0},{10,2},{8,4},{1,6},{3,14},{5,12},{7,10},{15,8},{13,1},{11,3... | collective-permute-start | bytes 4718600 | tf_op jit(solution)/shard_map/ppermute | solution.py:96
  6.4 1.9 %collective-permute-start.3 = (bf16[1024,768]{1,0:T(8,128)(2,1)S(1)}, bf16[1024,768]{1,0:T(8,128)(2,1)S(1)}, u32[]{:S(2)}, u32[]{:S(2)}) collective-permute-start(bf16[1024,768]{1,0:T(8,128)(2,1)S(1)} %bitcast_select_fusion), channel_id=1, source_target_pairs={{9,0},{0,2},{2,4},{4,6},{6,14},{14,12},{12,10},{10,8},{8,1},{1,3},... | collective-permute-start | bytes 4718600 | tf_op jit(solution)/shard_map/ppermute | solution.py:96
  8.3 0.7 collective-permute-start.2
  9.0 0.6 multiply_reduce_fusion.4
  10.7 0.7 fusion.3
  11.4 27.7 %collective-permute-done = bf16[1024,768]{1,0:T(8,128)(2,1)S(1)} collective-permute-done((bf16[1024,768]{1,0:T(8,128)(2,1)S(1)}, bf16[1024,768]{1,0:T(8,128)(2,1)S(1)}, u32[]{:S(2)}, u32[]{:S(2)}) %collective-permute-start) | collective-permute-done | bytes 1572896 | tf_op jit(solution)/shard_map/ppermute | solution.py:96
  39.5 3.9 %collective-permute-done.1 = bf16[1024,768]{1,0:T(8,128)(2,1)S(1)} collective-permute-done((bf16[1024,768]{1,0:T(8,128)(2,1)S(1)}, bf16[1024,768]{1,0:T(8,128)(2,1)S(1)}, u32[]{:S(2)}, u32[]{:S(2)}) %collective-permute-start.1) | collective-permute-done | bytes 1572896 | tf_op jit(solution)/shard_map/ppermute | solution.py:96
  43.9 31.2 %collective-permute-done.3 = bf16[1024,768]{1,0:T(8,128)(2,1)S(1)} collective-permute-done((bf16[1024,768]{1,0:T(8,128)(2,1)S(1)}, bf16[1024,768]{1,0:T(8,128)(2,1)S(1)}, u32[]{:S(2)}, u32[]{:S(2)}) %collective-permute-start.3) | collective-permute-done | bytes 1572896 | tf_op jit(solution)/shard_map/ppermute | solution.py:96
  80.2 0.6 convolution_multiply_fusion.6
  80.8 0.6 convolution_multiply_fusion.3
  81.5 0.6 convolution_multiply_fusion
  82.1 0.6 convolution_multiply_fusion.4
  82.7 0.6 convolution_multiply_fusion.1
  83.3 0.6 convolution_multiply_fusion.2
  84.0 2.3 %fusion.17 = (f32[512]{0:T(512)S(1)}, f32[512]{0:T(512)S(1)}, f32[512]{0:T(512)S(1)}, f32[512]{0:T(512)S(1)}, f32[512]{0:T(512)S(1)}, /*index=5*/f32[512]{0:T(51...) fusion(f32[512]{0:T(512)S(1)} %slice-done, ...), kind=kOutput, calls=%fused_computation.70 | convolution fusion | flops 412083200 | bytes 7907328 | tf_op jit(solution)/shard_map/dot_general | solution.py:72
  86.3 1.7 %collective-permute-start.7 = (f32[1024]{0:T(1024)S(1)}, f32[1024]{0:T(1024)S(1)}, u32[]{:S(2)}, u32[]{:S(2)}) collective-permute-start(f32[1024]{0:T(1024)S(1)} %pad_maximum_fusion.3), channel_id=1, source_target_pairs={{0,9},{2,0},{4,2},{6,4},{14,6},{12,14},{10,12},{8,10},{1,8},{3,1},... | collective-permute-start | bytes 12296 | tf_op jit(solution)/shard_map/ppermute | solution.py:103
  88.9 1.5 %collective-permute-start.6 = (f32[1024]{0:T(1024)S(1)}, f32[1024]{0:T(1024)S(1)}, u32[]{:S(2)}, u32[]{:S(2)}) collective-permute-start(f32[1024]{0:T(1024)S(1)} %pad_maximum_fusion.2), channel_id=1, source_target_pairs={{0,1},{2,3},{4,5},{6,7},{14,15},{12,13},{10,11},{8,9},{1,0},{3,2},... | collective-permute-start | bytes 12296 | tf_op jit(solution)/shard_map/ppermute | solution.py:103
  90.8 0.4 fusion.150
  91.3 3.2 %collective-permute-start.5 = (f32[1024]{0:T(1024)S(1)}, f32[1024]{0:T(1024)S(1)}, u32[]{:S(2)}, u32[]{:S(2)}) collective-permute-start(f32[1024]{0:T(1024)S(1)} %pad_maximum_fusion.1), channel_id=1, source_target_pairs={{0,12},{2,10},{4,8},{6,1},{14,3},{12,5},{10,7},{8,15},{1,13},{3,11... | collective-permute-start | bytes 12296 | tf_op jit(solution)/shard_map/ppermute | solution.py:103
  95.5 0.7 exponential_reduce_fusion
  96.7 1.4 %collective-permute-done.4 = f32[1024]{0:T(1024)S(1)} collective-permute-done((f32[1024]{0:T(1024)S(1)}, f32[1024]{0:T(1024)S(1)}, u32[]{:S(2)}, u32[]{:S(2)}) %collective-permute-start.4) | collective-permute-done | bytes 4128 | tf_op jit(solution)/shard_map/ppermute | solution.py:103
  98.1 0.6 fusion.154
  98.7 1.3 %broadcast_in_dim.44 = f32[128,1,1]{2,1,0:T(1,128)} broadcast(f32[]{:T(128)} %get-tuple-element.97), dimensions={} | broadcast | bytes 516 | tf_op jit(solution)/shard_map/broadcast_in_dim | solution.py:67
  100.0 8.2 %all-to-all-start = ((f32[128,1,1]{2,1,0:T(1,128)}), f32[128,1,1]{2,1,0:T(1,128)S(1)}, u32[]{:S(2)}, u32[]{:S(2)}) async-start(f32[128,1,1]{2,1,0:T(1,128)} %broadcast_in_dim.44), calls=%async_computation | async-start | bytes 131072 | tf_op jit(solution)/shard_map/all_to_all | solution.py:67
  108.3 9.5 %all-to-all-done = f32[128,1,1]{2,1,0:T(1,128)S(1)} async-done(((f32[128,1,1]{2,1,0:T(1,128)}), f32[128,1,1]{2,1,0:T(1,128)S(1)}, u32[]{:S(2)}, u32[]{:S(2)}) %all-to-all-start) | async-done | bytes 544 | tf_op jit(solution)/shard_map/all_to_all | solution.py:67
  117.8 0.7 reduce_sum.721
  119.3 0.6 gather_fusion.1
  119.8 0.7 select_bitcast_fusion
  (92 shorter events, 10.0 us)
Async XLA Ops:
  0.0 1.7 %copy-start = (bf16[1024,768]{1,0:T(8,128)(2,1)S(1)}, bf16[1024,768]{1,0:T(8,128)(2,1)}, u32[]{:S(2)}) copy-start(bf16[1024,768]{1,0:T(8,128)(2,1)} %param.2) | copy-start | bytes 4718596
  2.6 36.5 %collective-permute-start = (bf16[1024,768]{1,0:T(8,128)(2,1)S(1)}, bf16[1024,768]{1,0:T(8,128)(2,1)S(1)}, u32[]{:S(2)}, u32[]{:S(2)}) collective-permute-start(bf16[1024,768]{1,0:T(8,128)(2,1)S(1)} %bitcast_select_fusion), channel_id=1, source_target_pairs={{2,0},{4,2},{6,4},{14,6},{12,14},{10,12},{8,10},{1,8},{3,1},{5,3},... | collective-permute-start | bytes 4718600 | tf_op jit(solution)/shard_map/ppermute | solution.py:96
  3.8 39.7 %collective-permute-start.1 = (bf16[1024,768]{1,0:T(8,128)(2,1)S(1)}, bf16[1024,768]{1,0:T(8,128)(2,1)S(1)}, u32[]{:S(2)}, u32[]{:S(2)}) collective-permute-start(bf16[1024,768]{1,0:T(8,128)(2,1)S(1)} %bitcast_select_fusion), channel_id=1, source_target_pairs={{12,0},{10,2},{8,4},{1,6},{3,14},{5,12},{7,10},{15,8},{13,1},{11,3... | collective-permute-start | bytes 4718600 | tf_op jit(solution)/shard_map/ppermute | solution.py:96
  6.4 68.6 %collective-permute-start.3 = (bf16[1024,768]{1,0:T(8,128)(2,1)S(1)}, bf16[1024,768]{1,0:T(8,128)(2,1)S(1)}, u32[]{:S(2)}, u32[]{:S(2)}) collective-permute-start(bf16[1024,768]{1,0:T(8,128)(2,1)S(1)} %bitcast_select_fusion), channel_id=1, source_target_pairs={{9,0},{0,2},{2,4},{4,6},{6,14},{14,12},{12,10},{10,8},{8,1},{1,3},... | collective-permute-start | bytes 4718600 | tf_op jit(solution)/shard_map/ppermute | solution.py:96
  8.3 67.2 %collective-permute-start.2 = (bf16[1024,768]{1,0:T(8,128)(2,1)S(1)}, bf16[1024,768]{1,0:T(8,128)(2,1)S(1)}, u32[]{:S(2)}, u32[]{:S(2)}) collective-permute-start(bf16[1024,768]{1,0:T(8,128)(2,1)S(1)} %bitcast_select_fusion), channel_id=1, source_target_pairs={{1,0},{3,2},{5,4},{7,6},{15,14},{13,12},{11,10},{9,8},{0,1},{2,3},... | collective-permute-start | bytes 4718600 | tf_op jit(solution)/shard_map/ppermute | solution.py:96
  39.5 35.9 %copy-start.1 = (f32[1024]{0:T(1024)}, f32[1024]{0:T(1024)S(1)}, u32[]{:S(2)}) copy-start(f32[1024]{0:T(1024)S(1)} %multiply_reduce_fusion.3) | copy-start | bytes 12292
  43.8 32.0 %copy-start.2 = (f32[1024]{0:T(1024)}, f32[1024]{0:T(1024)S(1)}, u32[]{:S(2)}) copy-start(f32[1024]{0:T(1024)S(1)} %multiply_reduce_fusion.2) | copy-start | bytes 12292
  75.4 1.4 %copy-start.3 = (f32[1024]{0:T(1024)}, f32[1024]{0:T(1024)S(1)}, u32[]{:S(2)}) copy-start(f32[1024]{0:T(1024)S(1)} %multiply_reduce_fusion) | copy-start | bytes 12292
  83.3 0.7 slice-start
  83.3 0.7 slice-start.1
  83.3 0.7 slice-start.2
  86.3 10.4 %collective-permute-start.7 = (f32[1024]{0:T(1024)S(1)}, f32[1024]{0:T(1024)S(1)}, u32[]{:S(2)}, u32[]{:S(2)}) collective-permute-start(f32[1024]{0:T(1024)S(1)} %pad_maximum_fusion.3), channel_id=1, source_target_pairs={{0,9},{2,0},{4,2},{6,4},{14,6},{12,14},{10,12},{8,10},{1,8},{3,1},... | collective-permute-start | bytes 12296 | tf_op jit(solution)/shard_map/ppermute | solution.py:103
  88.9 7.8 %collective-permute-start.6 = (f32[1024]{0:T(1024)S(1)}, f32[1024]{0:T(1024)S(1)}, u32[]{:S(2)}, u32[]{:S(2)}) collective-permute-start(f32[1024]{0:T(1024)S(1)} %pad_maximum_fusion.2), channel_id=1, source_target_pairs={{0,1},{2,3},{4,5},{6,7},{14,15},{12,13},{10,11},{8,9},{1,0},{3,2},... | collective-permute-start | bytes 12296 | tf_op jit(solution)/shard_map/ppermute | solution.py:103
  91.3 5.4 %collective-permute-start.5 = (f32[1024]{0:T(1024)S(1)}, f32[1024]{0:T(1024)S(1)}, u32[]{:S(2)}, u32[]{:S(2)}) collective-permute-start(f32[1024]{0:T(1024)S(1)} %pad_maximum_fusion.1), channel_id=1, source_target_pairs={{0,12},{2,10},{4,8},{6,1},{14,3},{12,5},{10,7},{8,15},{1,13},{3,11... | collective-permute-start | bytes 12296 | tf_op jit(solution)/shard_map/ppermute | solution.py:103
  95.0 3.1 %collective-permute-start.4 = (f32[1024]{0:T(1024)S(1)}, f32[1024]{0:T(1024)S(1)}, u32[]{:S(2)}, u32[]{:S(2)}) collective-permute-start(f32[1024]{0:T(1024)S(1)} %pad_maximum_fusion), channel_id=1, source_target_pairs={{0,2},{2,4},{4,6},{6,14},{14,12},{12,10},{10,8},{8,1},{1,3},{3,5},... | collective-permute-start | bytes 12296 | tf_op jit(solution)/shard_map/ppermute | solution.py:103
  100.0 17.8 %all-to-all-start = ((f32[128,1,1]{2,1,0:T(1,128)}), f32[128,1,1]{2,1,0:T(1,128)S(1)}, u32[]{:S(2)}, u32[]{:S(2)}) async-start(f32[128,1,1]{2,1,0:T(1,128)} %broadcast_in_dim.44), calls=%async_computation | async-start | bytes 131072 | tf_op jit(solution)/shard_map/all_to_all | solution.py:67
